TPU v7x, 128 devices: a whole 4x4x4 slice. The times are simulated.
128 devices in a mesh: req: 16 (over y, z), mlp: 8 (over x, core).
Axes of the slice: x: 4, y: 4, z: 4, core: 2. Of those that a mesh axis runs over, the one named last changes fastest.
Arguments:
- tokens: bfloat16 [32768, 1536], P(('req', 'mlp')), may hold values from -6 to 6
- attn_gain: float32 [1536], replicated, may hold values from 0.1 to 1.9
- w_query: bfloat16 [1536, 1536], replicated, may hold values from -0.15625 to 0.15625
- w_keyval: bfloat16 [1536, 256], replicated, may hold values from -0.15625 to 0.15625
- w_out: bfloat16 [1536, 1536], replicated, may hold values from -0.15625 to 0.15625
- ffn_gain: float32 [1536], replicated, may hold values from 0.1 to 1.9
- w_gate: bfloat16 [1536, 4608], P('req', 'mlp'), may hold values from -0.15625 to 0.15625
- w_up: bfloat16 [1536, 4608], P('req', 'mlp'), may hold values from -0.15625 to 0.15625
- w_down: bfloat16 [1536, 4608], P('req', 'mlp'), may hold values from -0.09375 to 0.09375
- prefix_kv: bfloat16 [2, 128, 512, 256], P(None, 'req'), may hold values from -60 to 60, as said below
- own_prefix: bfloat16 [16, 512, 256], P('req'), may hold values from -60 to 60, as said below
- leaf_parent: int32 [16], replicated, may hold values from 0 to 127
- node_parent: int32 [128], replicated, may hold values from 0 to 127
- seg_lengths: int32 [3, 128], replicated, may hold values from 1 to 512
Outputs:
- layer_out: bfloat16 [32768, 1536], P(('req', 'mlp'))
Inputs may be any that keep to these rules, and one draw needn't show every extreme that they name: `prefix_kv`: columns below 128 are keys, the rest values. `own_prefix`: columns below 128 are keys, the rest values.
All inputs are finite; a program needn't handle non-finite values.
Results may differ from a plain program's by a relative error of at most 0.018.
Values may be sent and summed in bfloat16 or wider, within the bound.
No kernel may reach another device: no remote copies, remote signals or barrier semaphores. Data moves between devices by JAX's collectives and lax.ppermute only.
A program may use at most 192 MiB of HBM per device.

v0:
```python
import jax
import jax.numpy as jnp
from jax import lax
from jax.sharding import PartitionSpec as P

HEADS = 12
HD = 128
WINDOW = 1024
EPS = 1e-06


def rms_scale(values, gain):
    wide = values.astype(jnp.float32)
    return wide * lax.rsqrt(jnp.mean(wide * wide, axis=-1, keepdims=True) + EPS) * gain


def rotate(values, where_at):
    half_dim = values.shape[-1] // 2
    freqs = 10000.0 ** (-jnp.arange(half_dim, dtype=jnp.float32) / half_dim)
    angles = where_at.astype(jnp.float32)[:, None] * freqs[None, :]
    cosine = jnp.cos(angles)[:, None, :]
    sine = jnp.sin(angles)[:, None, :]
    first = values[..., :half_dim]
    second = values[..., half_dim:]
    return jnp.concatenate([first * cosine - second * sine, first * sine + second * cosine], -1)


def body(
    tokens,
    attn_gain,
    w_query,
    w_keyval,
    w_out,
    ffn_gain,
    w_gate,
    w_up,
    w_down,
    prefix_kv,
    own_prefix,
    leaf_parent,
    node_parent,
    seg_lengths,
):
    tok_rows = tokens.shape[0]
    mine = lax.axis_index("req")
    n_mlp = lax.axis_size("mlp")
    position_group = lax.axis_index("mlp")
    node_dev = prefix_kv.shape[1]
    seg_slot = prefix_kv.shape[2]
    share = seg_slot // n_mlp
    leaf = leaf_parent[mine]
    upper = node_parent[leaf]
    len_zero = seg_lengths[0, upper]
    len_one = seg_lengths[1, leaf]
    len_two = seg_lengths[2, mine]
    total = len_zero + len_one + len_two
    ff_cols = w_gate.shape[1]
    packed = lax.all_gather(jnp.concatenate([w_gate, w_up, w_down], 1), "req", axis=0, tiled=True)
    down_full = packed[:, 2 * ff_cols :]
    level_zero = node_parent[leaf_parent]
    wanted = jnp.stack([level_zero, leaf_parent], 1)
    local_slot = wanted % node_dev
    my_rows = lax.dynamic_slice_in_dim(prefix_kv, position_group * share, share, 2)
    outgoing = my_rows[jnp.arange(2)[None, :], local_slot]
    arrived = lax.all_to_all(outgoing, "req", split_axis=0, concat_axis=0, tiled=True)
    owners = wanted[mine] // node_dev
    my_part = arrived[owners, jnp.arange(2)]
    levels = lax.all_gather(my_part, "mlp", axis=1, tiled=True)
    query_at = total + position_group * tok_rows + jnp.arange(tok_rows, dtype=jnp.int32)
    normed = rms_scale(tokens, attn_gain).astype(jnp.bfloat16)
    query_full = jnp.dot(normed, w_query, preferred_element_type=jnp.float32).reshape(
        tok_rows, HEADS, HD
    )
    queries = (rotate(query_full, query_at) * HD ** (-0.5)).astype(jnp.bfloat16)
    keyval_full = jnp.dot(normed, w_keyval, preferred_element_type=jnp.float32)
    new_keys = rotate(keyval_full[:, None, :HD], query_at)[:, 0].astype(jnp.bfloat16)
    new_vals = keyval_full[:, HD:].astype(jnp.bfloat16)
    new_keyval = jnp.concatenate([new_keys, new_vals], 1)
    piece = lax.all_gather(new_keyval, "mlp", axis=0, tiled=True)
    sources = jnp.concatenate([levels[0], levels[1], own_prefix[0], piece], 0)
    seq_len = 3 * seg_slot + piece.shape[0]
    span = WINDOW + tok_rows
    first = jnp.clip(total + position_group * tok_rows - WINDOW, 0, seq_len - span)
    key_at = first + jnp.arange(span, dtype=jnp.int32)
    len_cut = len_zero + len_one
    source_row = jnp.where(
        key_at < len_zero,
        key_at,
        jnp.where(
            key_at < len_cut,
            key_at - len_zero + seg_slot,
            jnp.where(
                key_at < total, key_at - len_cut + 2 * seg_slot, key_at - total + 3 * seg_slot
            ),
        ),
    )
    window = jnp.take(sources, source_row, axis=0, mode="clip")
    spacing = query_at[:, None] - key_at[None, :]
    allowed = ((spacing >= 0) & (spacing < WINDOW))[:, None, :]
    scores = jnp.einsum("thd,kd->thk", queries, window[:, :HD], preferred_element_type=jnp.float32)
    top = jnp.max(jnp.where(allowed, scores, -jnp.inf), axis=-1, keepdims=True)
    weights = jnp.where(allowed, jnp.exp(scores - top), 0.0)
    denom = jnp.sum(weights, axis=-1)
    mixed = jnp.einsum(
        "thk,kd->thd",
        weights.astype(jnp.bfloat16),
        window[:, HD:],
        preferred_element_type=jnp.float32,
    )
    context = (mixed / denom[..., None]).reshape(tok_rows, HEADS * HD).astype(jnp.bfloat16)
    attn_out = jnp.dot(context, w_out, preferred_element_type=jnp.float32)
    resid = (tokens.astype(jnp.float32) + attn_out).astype(jnp.bfloat16)
    ffn_in = rms_scale(resid, ffn_gain).astype(jnp.bfloat16)
    all_rows = lax.all_gather(ffn_in, "mlp", axis=0, tiled=True)
    gate_up = jnp.dot(all_rows, packed[:, : 2 * ff_cols], preferred_element_type=jnp.float32)
    gate = gate_up[:, :ff_cols]
    upward = gate_up[:, ff_cols:]
    hidden = (jax.nn.gelu(gate, approximate=True) * upward).astype(jnp.bfloat16)
    summed = lax.psum_scatter(
        lax.dot_general(
            hidden, down_full, (((1,), (1,)), ((), ())), preferred_element_type=jnp.float32
        ).astype(jnp.bfloat16),
        "mlp",
        scatter_dimension=0,
        tiled=True,
    ).astype(jnp.float32)
    return (resid.astype(jnp.float32) + summed).astype(jnp.bfloat16)


def solution(mesh):
    return jax.shard_map(
        body,
        mesh=mesh,
        in_specs=(
            P(("req", "mlp"), None),
            P(),
            P(),
            P(),
            P(),
            P(),
            P("req", "mlp"),
            P("req", "mlp"),
            P("req", "mlp"),
            P(None, "req", None, None),
            P("req", None, None),
            P(),
            P(),
            P(),
        ),
        out_specs=P(("req", "mlp"), None),
        check_vma=False,
    )
```

profile of v0, /device:TPU:1, one launch (start us, length us, event | category | flops | bytes accessed | tf_op | source)
XLA Modules:
  0.0 221.3 jit_solution(13196897716380005611)
XLA Ops:
  6.5 1.3 dynamic_slice.21
  9.8 1.2 dynamic_slice.22
  12.4 1.4 fusion.29
  13.8 1.8 fusion.37
  22.9 1.6 gather_fusion.1
  24.5 8.6 %all-to-all-start = ((bf16[16,2,64,256]{3,2,1,0:T(8,128)(2,1)}), bf16[16,2,64,256]{3,2,1,0:T(8,128)(2,1)}, u32[]{:S(2)}, u32[]{:S(2)}) async-start(bf16[16,2,64,256]{3,2,1,0:T(8,128)(2,1)} %bitcast.8), calls=%async_computation | async-start | bytes 2097152 | tf_op jit(solution)/shard_map/all_to_all | solution.py:65
  35.2 4.4 %fusion.39 = f32[256,1536]{0,1:T(8,128)S(1)} fusion(bf16[1536,1536]{1,0:T(8,128)(2,1)} %param.16, bf16[256,1536]{1,0:T(8,128)(2,1)S(1)} %copy-done.3, f32[1536]{0:T(1024)S(1)} %copy-done.13, f32[256]{0:T(256)S(1)} %add_rsqrt_fusion.1), kind=kOutput, calls=%fused_computation.55 | convolution fusion | flops 1209532416 | bytes 7085056 | tf_op jit(solution)/shard_map/dot_general | solution.py:71
  41.3 1.6 copy.40
  43.0 1.7 copy.41
  45.3 3.5 %multiply_subtract_fusion = (f32[256,12,64]{2,0,1:T(8,128)}, f32[256,12,64]{2,0,1:T(8,128)}) fusion(f32[256,12,64]{2,0,1:T(8,128)} %copy.41, f32[256,12,64]{2,0,1:T(8,128)S(1)} %copy.40, f32[256,64]{1,0:T(8,128)} %get-tuple-element.17, f32[256,64]{1,0:T(8,128)S(1)} %get-tuple-element.16), kind=kLoop, calls=%fused_computation.49 | loop fusion | flops 1179648 | bytes 3276800 | tf_op jit(solution)/shard_map/sub | solution.py:25
  49.9 1.8 gather_fusion.2
  51.8 15.5 %all_gather.12 = bf16[2,512,256]{2,0,1:T(2,128)(2,1)S(1)} all-gather(bf16[2,64,256]{2,0,1:T(2,128)(2,1)S(1)} %copy.33), channel_id=1, replica_groups=mesh['req'=16,'mlp'=8] {'mlp'}, dimensions={1}, use_global_device_ids=true | all-gather | bytes 589824 | tf_op jit(solution)/shard_map/all_gather | solution.py:68
  69.4 2.6 %pad_maximum_fusion = bf16[3584,256]{0,1:T(8,128)(2,1)} fusion(bf16[2048,256]{0,1:T(8,128)(2,1)} %all-gather.4.cloned.1.call-done, bf16[512,256]{0,1:T(8,128)(2,1)S(1)} %bitcast.59, bf16[512,256]{0,1:T(8,128)(2,1)S(1)} %bitcast.58, bf16[512,256]{0,1:T(8,128)(2,1)S(1)} %bitcast.57), kind=kLoop, calls=%fused_computation.38 | loop fusion | flops 7340032 | bytes 3670016 | tf_op jit(solution)/shard_map/concatenate | solution.py:80
  72.0 2.9 %copy.37 = bf16[3584,256]{1,0:T(8,128)(2,1)S(1)} copy(bf16[3584,256]{0,1:T(8,128)(2,1)} %pad_maximum_fusion) | data formatting | bytes 3670016 | tf_op jit(solution)/shard_map/concatenate | solution.py:80
  74.9 4.1 %gather_fusion.3 = bf16[1280,256]{1,0:T(8,128)(2,1)S(1)} fusion(bf16[3584,256]{1,0:T(8,128)(2,1)S(1)} %copy.37, s32[2048]{0:T(1024)S(1)} %pad_clamp_fusion), kind=kCustom, calls=%fused_computation.3 | custom fusion | bytes 1315840 | tf_op jit(solution)/shard_map/jit(_take)/gather | solution.py:97
  79.0 11.3 %fusion.66 = (f32[256,12]{0,1:T(8,128)S(1)}, bf16[256,12,1280]{2,0,1:T(8,128)(2,1)}) fusion(pred[256,1280]{1,0:T(8,128)(4,1)} %fusion.35, bf16[1280,256]{1,0:T(8,128)(2,1)S(1)} %gather_fusion.3, f32[256,12,64]{2,0,1:T(8,128)} %get-tuple-element.6, f32[256,12,64]{2,0,1:T(8,128)} %get-tuple-element.5), kind=kOutput, calls=%fused_computation.116 | convolution fusion | flops 2035287296 | bytes 15478784 | tf_op jit(solution)/shard_map/sub | solution.py:102
  90.3 6.0 %divide_convert_fusion = bf16[256,12,128]{0,2,1:T(8,128)(2,1)S(1)} fusion(bf16[256,12,1280]{2,0,1:T(8,128)(2,1)} %get-tuple-element.19, f32[256,12]{0,1:T(8,128)S(1)} %get-tuple-element.18, bf16[1280,256]{1,0:T(8,128)(2,1)S(1)} %gather_fusion.3), kind=kOutput, calls=%fused_computation.47 | convolution fusion | flops 1007419392 | bytes 8994816 | tf_op jit(solution)/shard_map/thk,kd->thd/dot_general | solution.py:104
  96.4 3.9 %multiply_reduce_fusion = (f32[256]{0:T(256)S(1)}, f32[256,1536]{1,0:T(8,128)S(1)}) fusion(bf16[256,1536]{0,1:T(8,128)(2,1)S(1)} %bitcast.55, bf16[1536,1536]{1,0:T(8,128)(2,1)} %param.18, bf16[256,1536]{1,0:T(8,128)(2,1)S(1)} %copy-done.3), kind=kOutput, calls=%fused_computation.46 | convolution fusion | flops 1210318592 | bytes 7865344 | tf_op jit(solution)/shard_map/dot_general | solution.py:111
  101.7 5.8 %all-gather.8.cloned.1.call-done = bf16[1536,1728]{1,0:T(8,128)(2,1)} async-done(((bf16[96,1728]{1,0:T(8,128)(2,1)}), bf16[1536,1728]{1,0:T(8,128)(2,1)}) %all-gather.8.cloned.1.call-update) | async-done | bytes 5308432 | tf_op jit(solution)/shard_map/all_gather | solution.py:58
  107.5 42.6 %all-gather.6.cloned.1.call-done = bf16[2048,1536]{1,0:T(8,128)(2,1)} async-done(((bf16[256,1536]{1,0:T(8,128)(2,1)}), bf16[2048,1536]{1,0:T(8,128)(2,1)}) %all-gather.6.cloned.1.call-update) | async-done | bytes 6291472 | tf_op jit(solution)/shard_map/all_gather | solution.py:114
  150.1 11.1 %fusion.17 = f32[2048,1152]{0,1:T(8,128)S(1)} fusion(bf16[2048,1536]{1,0:T(8,128)(2,1)} %all-gather.6.cloned.1.call-done, bf16[1536,1728]{1,0:T(8,128)(2,1)} %all-gather.8.cloned.1.call-done), kind=kOutput, calls=%fused_computation.23 | convolution fusion | flops 7247757312 | bytes 19267584 | tf_op jit(solution)/shard_map/dot_general | solution.py:115
  161.2 9.6 %convolution_convert_fusion = bf16[2048,1536]{1,0:T(8,128)(2,1)} fusion(f32[2048,1152]{0,1:T(8,128)S(1)} %fusion.17, bf16[1536,1728]{1,0:T(8,128)(2,1)} %all-gather.8.cloned.1.call-done), kind=kOutput, calls=%fused_computation.12 | convolution fusion | flops 3638820864 | bytes 17694720 | tf_op jit(solution)/shard_map/dot_general | solution.py:120
  170.8 41.7 %reduce-scatter.2.cloned.1.call-done = bf16[256,1536]{1,0:T(8,128)(2,1)} async-done(((bf16[2048,1536]{1,0:T(8,128)(2,1)}), bf16[256,1536]{1,0:T(8,128)(2,1)}) %reduce-scatter.2.cloned.1.call-update) | async-done | bytes 786448 | tf_op jit(solution)/shard_map/reduce_scatter | solution.py:119
  212.5 2.2 add_convert_fusion
  (72 shorter events, 13.7 us)
Async XLA Ops:
  6.5 7.2 %copy-start = (bf16[1536,256]{1,0:T(8,128)(2,1)S(1)}, bf16[1536,256]{1,0:T(8,128)(2,1)}, u32[]{:S(2)}) copy-start(bf16[1536,256]{1,0:T(8,128)(2,1)} %param.17) | copy-start | bytes 2359300
  6.5 9.8 %copy-start.11 = (s32[3,128]{1,0:T(4,128)S(1)}, s32[3,128]{1,0:T(4,128)}, u32[]{:S(2)}) copy-start(s32[3,128]{1,0:T(4,128)} %param.27) | copy-start | bytes 4612
  6.5 62.8 %all-gather.4.cloned.1.call-start = ((), (), s32[]{:S(2)}) async-start(), calls=%async_computation.2 | async-start | bytes 1179648 | tf_op jit(solution)/shard_map/all_gather | solution.py:79
  13.7 6.3 %copy-start.5 = (bf16[96,576]{1,0:T(8,128)(2,1)S(1)}, bf16[96,576]{1,0:T(8,128)(2,1)}, u32[]{:S(2)}) copy-start(bf16[96,576]{1,0:T(8,128)(2,1)} %param.20) | copy-start | bytes 331780
  13.7 6.3 %copy-start.6 = (bf16[96,576]{1,0:T(8,128)(2,1)S(1)}, bf16[96,576]{1,0:T(8,128)(2,1)}, u32[]{:S(2)}) copy-start(bf16[96,576]{1,0:T(8,128)(2,1)} %param.21) | copy-start | bytes 331780
  13.7 6.3 %copy-start.7 = (bf16[96,576]{1,0:T(8,128)(2,1)S(1)}, bf16[96,576]{1,0:T(8,128)(2,1)}, u32[]{:S(2)}) copy-start(bf16[96,576]{1,0:T(8,128)(2,1)} %param.22) | copy-start | bytes 331780
  13.8 7.1 %copy-start.10 = (s32[16]{0:T(128)S(1)}, s32[16]{0:T(128)}, u32[]{:S(2)}) copy-start(s32[16]{0:T(128)} %param.25) | copy-start | bytes 196
  13.8 7.2 %copy-start.2 = (s32[128]{0:T(128)S(1)}, s32[128]{0:T(128)}, u32[]{:S(2)}) copy-start(s32[128]{0:T(128)} %param.26) | copy-start | bytes 1540
  19.9 87.6 %all-gather.8.cloned.1.call-start = ((), (), s32[]{:S(2)}) async-start(), calls=%async_computation.4 | async-start | bytes 5849088 | tf_op jit(solution)/shard_map/all_gather | solution.py:58
  22.9 12.3 %copy-start.3 = (bf16[256,1536]{1,0:T(8,128)(2,1)S(1)}, bf16[256,1536]{1,0:T(8,128)(2,1)}, u32[]{:S(2)}) copy-start(bf16[256,1536]{1,0:T(8,128)(2,1)} %param.14) | copy-start | bytes 2359300
  22.9 12.3 %copy-start.13 = (f32[1536]{0:T(1024)S(1)}, f32[1536]{0:T(1024)}, u32[]{:S(2)}) copy-start(f32[1536]{0:T(1024)} %param.15) | copy-start | bytes 18436
  24.5 25.4 %all-to-all-start = ((bf16[16,2,64,256]{3,2,1,0:T(8,128)(2,1)}), bf16[16,2,64,256]{3,2,1,0:T(8,128)(2,1)}, u32[]{:S(2)}, u32[]{:S(2)}) async-start(bf16[16,2,64,256]{3,2,1,0:T(8,128)(2,1)} %bitcast.8), calls=%async_computation | async-start | bytes 2097152 | tf_op jit(solution)/shard_map/all_to_all | solution.py:65
  33.2 116.9 %all-gather.6.cloned.1.call-start = ((), (), s32[]{:S(2)}) async-start(), calls=%async_computation.3 | async-start | bytes 7077888 | tf_op jit(solution)/shard_map/all_gather | solution.py:114
  39.6 1.6 copy-start.4
  45.3 3.5 %copy-start.12 = (s32[256]{0:T(256)S(1)}, s32[256]{0:T(256)}, u32[]{:S(2)}) copy-start(s32[256]{0:T(256)} %iota_add_fusion.1) | copy-start | bytes 3076
  45.3 4.6 %copy-start.9 = (s32[2]{0:T(128)S(1)}, s32[2]{0:T(128)}, u32[]{:S(2)}) copy-start(s32[2]{0:T(128)} %fusion.57) | copy-start | bytes 28
  96.4 4.0 %copy-start.8 = (f32[1536]{0:T(1024)S(1)}, f32[1536]{0:T(1024)}, u32[]{:S(2)}) copy-start(f32[1536]{0:T(1024)} %param.19) | copy-start | bytes 18436
  101.4 111.1 %reduce-scatter.2.cloned.1.call-start = ((), (), s32[]{:S(2)}) async-start(), calls=%async_computation.5 | async-start | bytes 7077888 | tf_op jit(solution)/shard_map/reduce_scatter | solution.py:119
  170.8 43.9 %copy-start.1 = (bf16[1536,256]{1,0:T(8,128)(2,1)S(1)}, bf16[1536,256]{1,0:T(8,128)(2,1)}, u32[]{:S(2)}) copy-start(bf16[1536,256]{1,0:T(8,128)(2,1)} %param.17) | copy-start | bytes 2359300
Sparse Core Ops, SparseCore 0:
  20.1 26.9 all-gather.3
  49.2 58.2 all-gather.7
  109.2 40.8 all-gather.5
  170.9 41.5 reduce-scatter.1
where the time goes:
time: 222 us; the launch traced here: 221 us
  waiting for transfers between devices  90.2 us (41%)
  matrix products  48.2 us (22%)
  local copies, waits for them, and re-layouts  23.2 us (10%)
  between operations  19.3 us (9%)
  other arithmetic  15.9 us (7%)
  blocking collectives  15.5 us (7%)
  starting transfers between devices  9 us (4%)
    all_gather x1, waiting for transfers between devices, body(): all_rows = lax.all_gather(ffn_in, 'mlp', axis=0, tiled=True)  42.6 us
    reduce_scatter x1, waiting for transfers between devices, body(): lax.psum_scatter(lax.dot_general(hidden, down_full, (((1,), (1,)), ((), (...  41.7 us
    all_gather x1, blocking collectives, body(): levels = lax.all_gather(my_part, 'mlp', axis=1, tiled=True)  15.5 us
    sub x1, matrix products, body(): weights = jnp.where(allowed, jnp.exp(scores - top), 0.0)  11.3 us
    dot_general x1, matrix products, body(): jnp.dot(all_rows, packed[:, :2 * ff_cols], preferred_element_type=jnp.flo...  11.1 us
    dot_general x1, matrix products, body(): lax.dot_general(hidden, down_full, (((1,), (1,)), ((), ())), preferred_el...  9.57 us
    all_to_all x1, starting transfers between devices, body(): lax.all_to_all(outgoing, 'req', split_axis=0, concat_axis=0, tiled=True)  8.65 us
    dot_general x1, matrix products, body(): jnp.einsum('thk,kd->thd', weights.astype(jnp.bfloat16), window[:, HD:], p...  6.03 us
  transfers between devices with their start and end apart: 5, of which 3 were waited for; matrix products, arithmetic and copies ran while one was open for 26% of the time, Pallas kernels for 0%

commit v1 on v0

--- a/solution.py
+++ b/solution.py
@@ -7,6 +7,14 @@
 HD = 128
 WINDOW = 1024
 EPS = 1e-06
+
+
+def begin_leaves(own_rows):
+    part_now = lax.axis_size("req")
+    answer = jnp.stack([own_rows] * part_now, axis=0)
+    spare = lax.all_to_all(answer, axis_name="req", split_axis=0, concat_axis=0)
+    extra = jnp.concatenate(spare, axis=0)
+    return extra
 
 
 def rms_scale(values, gain):
@@ -55,7 +63,7 @@
     len_two = seg_lengths[2, mine]
     total = len_zero + len_one + len_two
     ff_cols = w_gate.shape[1]
-    packed = lax.all_gather(jnp.concatenate([w_gate, w_up, w_down], 1), "req", axis=0, tiled=True)
+    packed = begin_leaves(jnp.concatenate([w_gate, w_up, w_down], 1))
     down_full = packed[:, 2 * ff_cols :]
     level_zero = node_parent[leaf_parent]
     wanted = jnp.stack([level_zero, leaf_parent], 1)

time: 222 us -> 240 us (1.081)
  blocking collectives: 15.5 us -> 85.3 us
  waiting for transfers between devices: 90.2 us -> 40.3 us
    all_to_all x0 -> x1, blocking collectives: none -> 68.8 us  [begin_leaves(): spare = lax.all_to_all(answer, axis_name='req', split_axis=0, concat_axis=0)]
    all_gather x1, waiting for transfers between devices: 42.6 us -> 0.01 us  [body(): all_rows = lax.all_gather(ffn_in, 'mlp', axis=0, tiled=True)]
    all_gather x1 -> x0, waiting for transfers between devices: 5.82 us -> none  [body(): lax.all_gather(jnp.concatenate([w_gate, w_up, w_down], 1), 'req', axis=0,...]
    unnamed x33 -> x31, local copies, waits for them, and re-layouts: 4.84 us -> 4.79 us
  transfers between devices with their start and end apart: 5 -> 4, of which waited for: 3 -> 1; matrix products, arithmetic and copies ran while one was open for 26% -> 10% of each run, Pallas kernels for 0% -> 0%
where the time goes in v1:
time: 240 us
  blocking collectives  85.3 us (36%)
  matrix products  48.1 us (20%)
  waiting for transfers between devices  40.3 us (17%)
  local copies, waits for them, and re-layouts  23 us (10%)
  between operations  19.3 us (8%)
  other arithmetic  14.9 us (6%)
  starting transfers between devices  8.73 us (4%)
    all_to_all x1, blocking collectives, begin_leaves(): spare = lax.all_to_all(answer, axis_name='req', split_axis=0, concat_axis=0)  68.8 us
    reduce_scatter x1, waiting for transfers between devices, body(): lax.psum_scatter(lax.dot_general(hidden, down_full, (((1,), (1,)), ((), (...  40.2 us
    all_gather x1, blocking collectives, body(): levels = lax.all_gather(my_part, 'mlp', axis=1, tiled=True)  16.5 us
    sub x1, matrix products, body(): weights = jnp.where(allowed, jnp.exp(scores - top), 0.0)  11.6 us
    dot_general x1, matrix products, body(): jnp.dot(all_rows, packed[:, :2 * ff_cols], preferred_element_type=jnp.flo...  11.1 us
    dot_general x1, matrix products, body(): lax.dot_general(hidden, down_full, (((1,), (1,)), ((), ())), preferred_el...  9.57 us
    all_to_all x1, starting transfers between devices, body(): lax.all_to_all(outgoing, 'req', split_axis=0, concat_axis=0, tiled=True)  8.65 us
    dot_general x1, matrix products, body(): jnp.einsum('thk,kd->thd', weights.astype(jnp.bfloat16), window[:, HD:], p...  5.92 us
  transfers between devices with their start and end apart: 4, of which 1 were waited for; matrix products, arithmetic and copies ran while one was open for 10% of the time, Pallas kernels for 0%

profile of v1, /device:TPU:1, one launch (start us, length us, event | category | flops | bytes accessed | tf_op | source)
XLA Modules:
  0.0 239.6 jit_solution(13214018051741657792)
XLA Ops:
  6.5 1.3 dynamic_slice.21
  9.8 1.2 dynamic_slice.22
  12.4 1.4 fusion.29
  13.8 1.7 fusion.37
  21.8 1.6 gather_fusion.1
  23.4 8.6 %all-to-all-start = ((bf16[16,2,64,256]{3,2,1,0:T(8,128)(2,1)}), bf16[16,2,64,256]{3,2,1,0:T(8,128)(2,1)}, u32[]{:S(2)}, u32[]{:S(2)}) async-start(bf16[16,2,64,256]{3,2,1,0:T(8,128)(2,1)} %bitcast.8), calls=%async_computation | async-start | bytes 2097152 | tf_op jit(solution)/shard_map/all_to_all | solution.py:73
  32.1 1.2 multiply_cosine_fusion
  33.5 4.4 %fusion.39 = f32[256,1536]{0,1:T(8,128)S(1)} fusion(bf16[1536,1536]{1,0:T(8,128)(2,1)} %param.16, bf16[256,1536]{1,0:T(8,128)(2,1)S(1)} %copy-done.3, f32[1536]{0:T(1024)S(1)} %copy-done.12, f32[256]{0:T(256)S(1)} %add_rsqrt_fusion.1), kind=kOutput, calls=%fused_computation.55 | convolution fusion | flops 1209532416 | bytes 7085056 | tf_op jit(solution)/shard_map/dot_general | solution.py:79
  39.1 1.6 copy.40
  40.7 1.6 copy.41
  43.0 3.6 %multiply_subtract_fusion = (f32[256,12,64]{2,0,1:T(8,128)}, f32[256,12,64]{2,0,1:T(8,128)}) fusion(f32[256,12,64]{2,0,1:T(8,128)} %copy.41, f32[256,12,64]{2,0,1:T(8,128)S(1)} %copy.40, f32[256,64]{1,0:T(8,128)} %get-tuple-element.17, f32[256,64]{1,0:T(8,128)S(1)} %get-tuple-element.16), kind=kLoop, calls=%fused_computation.49 | loop fusion | flops 1179648 | bytes 3276800 | tf_op jit(solution)/shard_map/sub | solution.py:33
  47.7 1.8 gather_fusion.2
  49.6 16.5 %all_gather.9 = bf16[2,512,256]{2,0,1:T(2,128)(2,1)S(1)} all-gather(bf16[2,64,256]{2,0,1:T(2,128)(2,1)S(1)} %copy.33), channel_id=1, replica_groups=mesh['req'=16,'mlp'=8] {'mlp'}, dimensions={1}, use_global_device_ids=true | all-gather | bytes 589824 | tf_op jit(solution)/shard_map/all_gather | solution.py:76
  68.2 2.6 %pad_maximum_fusion = bf16[3584,256]{0,1:T(8,128)(2,1)} fusion(bf16[2048,256]{0,1:T(8,128)(2,1)} %all-gather.3.cloned.1.call-done, bf16[512,256]{0,1:T(8,128)(2,1)S(1)} %bitcast.62, bf16[512,256]{0,1:T(8,128)(2,1)S(1)} %bitcast.61, bf16[512,256]{0,1:T(8,128)(2,1)S(1)} %bitcast.60), kind=kLoop, calls=%fused_computation.38 | loop fusion | flops 7340032 | bytes 3670016 | tf_op jit(solution)/shard_map/concatenate | solution.py:88
  70.8 2.9 %copy.37 = bf16[3584,256]{1,0:T(8,128)(2,1)S(1)} copy(bf16[3584,256]{0,1:T(8,128)(2,1)} %pad_maximum_fusion) | data formatting | bytes 3670016 | tf_op jit(solution)/shard_map/concatenate | solution.py:88
  73.7 4.1 %gather_fusion.3 = bf16[1280,256]{1,0:T(8,128)(2,1)S(1)} fusion(bf16[3584,256]{1,0:T(8,128)(2,1)S(1)} %copy.37, s32[2048]{0:T(1024)S(1)} %pad_clamp_fusion), kind=kCustom, calls=%fused_computation.3 | custom fusion | bytes 1315840 | tf_op jit(solution)/shard_map/jit(_take)/gather | solution.py:105
  77.8 11.6 %fusion.66 = (f32[256,12]{0,1:T(8,128)S(1)}, bf16[256,12,1280]{2,0,1:T(8,128)(2,1)}) fusion(pred[256,1280]{1,0:T(8,128)(4,1)} %fusion.35, bf16[1280,256]{1,0:T(8,128)(2,1)S(1)} %gather_fusion.3, f32[256,12,64]{2,0,1:T(8,128)} %get-tuple-element.6, f32[256,12,64]{2,0,1:T(8,128)} %get-tuple-element.5), kind=kOutput, calls=%fused_computation.116 | convolution fusion | flops 2035287296 | bytes 15478784 | tf_op jit(solution)/shard_map/sub | solution.py:110
  89.4 5.9 %divide_convert_fusion = bf16[256,12,128]{0,2,1:T(8,128)(2,1)S(1)} fusion(bf16[256,12,1280]{2,0,1:T(8,128)(2,1)} %get-tuple-element.19, f32[256,12]{0,1:T(8,128)S(1)} %get-tuple-element.18, bf16[1280,256]{1,0:T(8,128)(2,1)} %copy-done.4), kind=kOutput, calls=%fused_computation.47 | convolution fusion | flops 1007419392 | bytes 8990720 | tf_op jit(solution)/shard_map/thk,kd->thd/dot_general | solution.py:112
  95.3 3.8 %multiply_reduce_fusion = (f32[256]{0:T(256)S(1)}, f32[256,1536]{1,0:T(8,128)S(1)}) fusion(bf16[256,1536]{0,1:T(8,128)(2,1)S(1)} %bitcast.58, bf16[1536,1536]{1,0:T(8,128)(2,1)} %param.18, bf16[256,1536]{1,0:T(8,128)(2,1)S(1)} %copy-done.3), kind=kOutput, calls=%fused_computation.46 | convolution fusion | flops 1210318592 | bytes 7865344 | tf_op jit(solution)/shard_map/dot_general | solution.py:119
  101.1 68.8 %all_to_all.10 = bf16[16,96,1728]{2,1,0:T(8,128)(2,1)} all-to-all(bf16[16,96,1728]{2,1,0:T(8,128)(2,1)S(1)} %stack.40), channel_id=1, replica_groups=mesh['req'=16,'mlp'=8] {'req'}, dimensions={0} | all-to-all | bytes 10616832 | tf_op jit(solution)/shard_map/all_to_all | solution.py:15
  169.9 11.1 %fusion.17 = f32[2048,1152]{0,1:T(8,128)S(1)} fusion(bf16[2048,1536]{1,0:T(8,128)(2,1)} %all-gather.5.cloned.1.call-done, bf16[1536,1728]{1,0:T(8,128)(2,1)} %bitcast.56), kind=kOutput, calls=%fused_computation.23 | convolution fusion | flops 7247757312 | bytes 19267584 | tf_op jit(solution)/shard_map/dot_general | solution.py:123
  181.0 9.6 %convolution_convert_fusion = bf16[2048,1536]{1,0:T(8,128)(2,1)} fusion(f32[2048,1152]{0,1:T(8,128)S(1)} %fusion.17, bf16[1536,1728]{1,0:T(8,128)(2,1)} %bitcast.57), kind=kOutput, calls=%fused_computation.12 | convolution fusion | flops 3638820864 | bytes 17694720 | tf_op jit(solution)/shard_map/dot_general | solution.py:128
  190.6 40.2 %reduce-scatter.2.cloned.1.call-done = bf16[256,1536]{1,0:T(8,128)(2,1)} async-done(((bf16[2048,1536]{1,0:T(8,128)(2,1)}), bf16[256,1536]{1,0:T(8,128)(2,1)}) %reduce-scatter.2.cloned.1.call-update) | async-done | bytes 786448 | tf_op jit(solution)/shard_map/reduce_scatter | solution.py:127
  230.8 2.2 add_convert_fusion
  (69 shorter events, 10.9 us)
Async XLA Ops:
  6.5 7.2 %copy-start = (bf16[1536,256]{1,0:T(8,128)(2,1)S(1)}, bf16[1536,256]{1,0:T(8,128)(2,1)}, u32[]{:S(2)}) copy-start(bf16[1536,256]{1,0:T(8,128)(2,1)} %param.17) | copy-start | bytes 2359300
  6.5 9.6 %copy-start.11 = (s32[3,128]{1,0:T(4,128)S(1)}, s32[3,128]{1,0:T(4,128)}, u32[]{:S(2)}) copy-start(s32[3,128]{1,0:T(4,128)} %param.27) | copy-start | bytes 4612
  6.5 61.7 %all-gather.3.cloned.1.call-start = ((), (), s32[]{:S(2)}) async-start(), calls=%async_computation.3 | async-start | bytes 1179648 | tf_op jit(solution)/shard_map/all_gather | solution.py:87
  13.7 6.0 %copy-start.10 = (s32[16]{0:T(128)S(1)}, s32[16]{0:T(128)}, u32[]{:S(2)}) copy-start(s32[16]{0:T(128)} %param.25) | copy-start | bytes 196
  13.7 6.1 %copy-start.2 = (s32[128]{0:T(128)S(1)}, s32[128]{0:T(128)}, u32[]{:S(2)}) copy-start(s32[128]{0:T(128)} %param.26) | copy-start | bytes 1540
  21.8 11.8 %copy-start.3 = (bf16[256,1536]{1,0:T(8,128)(2,1)S(1)}, bf16[256,1536]{1,0:T(8,128)(2,1)}, u32[]{:S(2)}) copy-start(bf16[256,1536]{1,0:T(8,128)(2,1)} %param.14) | copy-start | bytes 2359300
  21.8 11.8 %copy-start.12 = (f32[1536]{0:T(1024)S(1)}, f32[1536]{0:T(1024)}, u32[]{:S(2)}) copy-start(f32[1536]{0:T(1024)} %param.15) | copy-start | bytes 18436
  23.4 24.3 %all-to-all-start = ((bf16[16,2,64,256]{3,2,1,0:T(8,128)(2,1)}), bf16[16,2,64,256]{3,2,1,0:T(8,128)(2,1)}, u32[]{:S(2)}, u32[]{:S(2)}) async-start(bf16[16,2,64,256]{3,2,1,0:T(8,128)(2,1)} %bitcast.8), calls=%async_computation | async-start | bytes 2097152 | tf_op jit(solution)/shard_map/all_to_all | solution.py:73
  32.0 137.8 %all-gather.5.cloned.1.call-start = ((), (), s32[]{:S(2)}) async-start(), calls=%async_computation.4 | async-start | bytes 7077888 | tf_op jit(solution)/shard_map/all_gather | solution.py:122
  37.9 1.1 copy-start.5
  77.8 11.6 %copy-start.4 = (bf16[1280,256]{1,0:T(8,128)(2,1)}, bf16[1280,256]{1,0:T(8,128)(2,1)S(1)}, u32[]{:S(2)}) copy-start(bf16[1280,256]{1,0:T(8,128)(2,1)S(1)} %gather_fusion.3) | copy-start | bytes 1966084
  95.3 3.9 %copy-start.9 = (f32[1536]{0:T(1024)S(1)}, f32[1536]{0:T(1024)}, u32[]{:S(2)}) copy-start(f32[1536]{0:T(1024)} %param.19) | copy-start | bytes 18436
  99.1 1.2 copy-start.6
  99.2 1.2 copy-start.7
  99.2 1.2 copy-start.8
  100.3 130.5 %reduce-scatter.2.cloned.1.call-start = ((), (), s32[]{:S(2)}) async-start(), calls=%async_computation.5 | async-start | bytes 7077888 | tf_op jit(solution)/shard_map/reduce_scatter | solution.py:127
  190.6 42.4 %copy-start.1 = (bf16[1536,256]{1,0:T(8,128)(2,1)S(1)}, bf16[1536,256]{1,0:T(8,128)(2,1)}, u32[]{:S(2)}) copy-start(bf16[1536,256]{1,0:T(8,128)(2,1)} %param.17) | copy-start | bytes 2359300
Sparse Core Ops, SparseCore 0:
  19.9 26.9 all-gather.2
  100.4 39.6 all-gather.4
  190.7 40.0 reduce-scatter.1
